TPU v7x, 512 devices: a whole 4x4x16 slice. The times are simulated.
512 devices in a mesh: ingest: 8 (over y, core), owner: 64 (over x, z).
Axes of the slice: x: 4, y: 4, z: 16, core: 2. Of those that a mesh axis runs over, the one named last changes fastest.
Arguments:
- frame_rows: bfloat16 [2112, 28, 1024], P('owner', None, 'ingest'), may hold values from -32 to 32
- route_owner: int32 [2112], P('owner'), may hold values from 0 to 63, as said below
- route_slot: int32 [2112], P('owner'), may hold values from 0 to 32, as said below
- frames: int32 [2112], P('owner'), may hold values from 1 to 28, as said below
- kv_cache: bfloat16 [2112, 8, 70, 256], P('owner', 'ingest'), may hold values from -250 to 250
- conv_cache: bfloat16 [2112, 8, 1024], P('owner', None, 'ingest'), may hold values from -5 to 5
- mig_owner: int32 [2048], P('owner'), may hold values from 0 to 63, as said below
- ln1_gain: float32 [1024], replicated, may hold values from 0.1 to 1.9
- w_qkv: bfloat16 [1024, 8, 384], P(None, 'ingest'), may hold values from -0.1875 to 0.1875
- w_out: bfloat16 [1024, 1024], P('ingest'), may hold values from -0.1875 to 0.1875
- ln2_gain: float32 [1024], replicated, may hold values from 0.1 to 1.9
- w_pw1: bfloat16 [1024, 2, 1024], P(None, None, 'ingest'), may hold values from -0.1875 to 0.1875
- dw_weight: bfloat16 [9, 1024], P(None, 'ingest'), may hold values from -2 to 2
- bn_scale: float32 [1024], P('ingest'), may hold values from 0.1 to 1.9
- bn_shift: float32 [1024], P('ingest'), may hold values from -2.5 to 2.5
- w_pw2: bfloat16 [1024, 1024], P('ingest'), may hold values from -0.1875 to 0.1875
Outputs:
- layer_out: bfloat16 [2112, 28, 1024], P('owner', None, 'ingest')
- kv_next: bfloat16 [2112, 8, 70, 256], P('owner', 'ingest')
- conv_next: bfloat16 [2112, 8, 1024], P('owner', None, 'ingest')
Inputs may be any that keep to these rules, and one draw needn't show every extreme that they name: `route_owner`: every owner receives exactly 33 utterances. The utterances that one source device along owner (a block of 33 rows in arrival order) sends to one owner number at most 1, and some source device reaches that number. `route_slot`: the utterances sent to one owner have distinct slots. Every owner holds an utterance with 28 new frames. The utterance in old slot 1 + j of an owner moves to slot 1 + j of owner mig_owner; the 32 utterances of one owner go to 32 different other owners, and every owner receives exactly one utterance for each j.
All inputs are finite; a program needn't handle non-finite values.
Results may differ from a plain program's by a relative error of at most 0.01.
Values may be sent and summed in bfloat16 or wider, within the bound.
No kernel may reach another device: no remote copies, remote signals or barrier semaphores. Data moves between devices by JAX's collectives and lax.ppermute only.
A program may use at most 64 MiB of HBM per device.

v0:
```python
import jax
import jax.numpy as jnp
from jax import lax
from jax.sharding import PartitionSpec as P

BLOCKS = 2
norm_eps = 1e-05


def normalize(values, gain_cols):
    model_width = values.shape[-1]
    row_mean = jnp.sum(values, axis=-1, keepdims=True) / model_width
    spread = jnp.sum(values * values, axis=-1, keepdims=True) / model_width - row_mean * row_mean
    return ((values - row_mean) * lax.rsqrt(spread + norm_eps) * gain_cols).astype(jnp.bfloat16)


def one_hot_rows(table, rows):
    return jnp.dot(table.astype(jnp.bfloat16), rows, preferred_element_type=jnp.float32).astype(
        jnp.bfloat16
    )


def grouped_terms(left_groups, right_groups):
    terms = jnp.einsum(
        "grc,gcn->grn", left_groups, right_groups, preferred_element_type=jnp.float32
    ).astype(jnp.bfloat16)
    return jnp.sum(terms.astype(jnp.float32), axis=0)


def shards(
    frame_rows,
    route_owner,
    route_slot,
    frames,
    kv_cache,
    conv_cache,
    mig_owner,
    ln1_gain,
    w_qkv,
    w_out,
    ln2_gain,
    w_pw1,
    dw_weight,
    bn_scale,
    bn_shift,
    w_pw2,
):
    owners = lax.axis_size("owner")
    groups = lax.axis_size("ingest")
    me = lax.axis_index("ingest")
    utterances, frame_span, local_width = frame_rows.shape
    model_width = w_qkv.shape[0]
    head_dim = w_qkv.shape[2] // 3
    cache_len = kv_cache.shape[2]
    conv_len = conv_cache.shape[1]
    taps = dw_weight.shape[0]
    horizon = frame_span // BLOCKS
    moving = mig_owner.shape[0]
    settled = utterances - moving
    lanes = 128
    w_out_full = lax.all_gather(w_out, "ingest", axis=0, tiled=True)
    w_pw2_cols = lax.all_to_all(
        w_pw2.reshape(local_width, groups, local_width).transpose(1, 0, 2),
        "ingest",
        split_axis=0,
        concat_axis=0,
        tiled=True,
    )
    dest = jnp.arange(owners, dtype=jnp.int32)
    frame_flat = frame_rows.reshape(utterances, frame_span * local_width)
    slot_tag = jnp.broadcast_to((route_slot + 1).astype(jnp.bfloat16)[:, None], (utterances, lanes))
    frame_send = one_hot_rows(
        dest[:, None] == route_owner[None, :], jnp.concatenate([frame_flat, slot_tag], axis=1)
    )
    kv_width = cache_len * 2 * head_dim
    conv_width = conv_len * local_width
    mover_tag = jnp.broadcast_to(
        (jnp.arange(moving, dtype=jnp.int32) + 1).astype(jnp.bfloat16)[:, None], (moving, lanes)
    )
    cache_rows = jnp.concatenate(
        [
            kv_cache[settled:].reshape(moving, kv_width),
            conv_cache[settled:].reshape(moving, conv_width),
            mover_tag,
        ],
        axis=1,
    )
    cache_send = one_hot_rows(dest[:, None] == mig_owner[None, :], cache_rows)
    frame_cols = frame_send.shape[1]
    arrived = lax.all_to_all(
        jnp.concatenate([frame_send, cache_send], axis=1),
        "owner",
        split_axis=0,
        concat_axis=0,
        tiled=True,
    )
    frame_part = frame_span * local_width
    got_slot = arrived[:, frame_part].astype(jnp.int32)
    slots = jnp.arange(utterances, dtype=jnp.int32)
    arranged = one_hot_rows(
        slots[:, None] + 1 == got_slot[None, :], arrived[:, :frame_part]
    ).reshape(utterances, frame_span, local_width)
    got_mover = arrived[:, frame_cols + kv_width + conv_width].astype(jnp.int32)
    movers = jnp.arange(moving, dtype=jnp.int32)
    moved = one_hot_rows(
        movers[:, None] + 1 == got_mover[None, :],
        arrived[:, frame_cols : frame_cols + kv_width + conv_width],
    )
    kv_state = jnp.concatenate(
        [
            kv_cache[:settled].reshape(settled, cache_len, 2 * head_dim),
            moved[:, :kv_width].reshape(moving, cache_len, 2 * head_dim),
        ],
        axis=0,
    )
    conv_state = jnp.concatenate(
        [conv_cache[:settled], moved[:, kv_width:].reshape(moving, conv_len, local_width)], axis=0
    )
    x_all = lax.all_gather(arranged, "ingest", axis=0, tiled=False)
    x_rows = x_all.transpose(1, 2, 0, 3).reshape(utterances, frame_span, model_width)
    x_rows = x_rows.astype(jnp.float32)
    normed = normalize(x_rows, ln1_gain)
    projected = jnp.dot(
        normed, w_qkv.reshape(model_width, 3 * head_dim), preferred_element_type=jnp.float32
    )
    queries = projected[..., :head_dim].astype(jnp.bfloat16)
    fresh = projected[..., head_dim:].astype(jnp.bfloat16)
    memory = jnp.concatenate([kv_state, fresh], axis=1)
    keys_total = memory.shape[1]
    scores = jnp.einsum(
        "sqd,skd->sqk", queries, memory[..., :head_dim], preferred_element_type=jnp.float32
    ) * head_dim ** (-0.5)
    frame_index = jnp.arange(frame_span, dtype=jnp.int32)
    block_of = frame_index // horizon
    low = block_of * horizon
    high = cache_len + jnp.minimum(frames[:, None], (block_of[None, :] + 1) * horizon)
    position = jnp.arange(keys_total, dtype=jnp.int32)
    live_keys = (position[None, None, :] >= low[None, :, None]) & (
        position[None, None, :] < high[:, :, None]
    )
    scores = jnp.where(live_keys, scores, -1e30)
    row_max = jnp.max(scores, axis=-1, keepdims=True)
    weights = jnp.exp(scores - row_max)
    probabilities = (weights / jnp.sum(weights, axis=-1, keepdims=True)).astype(jnp.bfloat16)
    context = jnp.einsum(
        "sqk,skd->sqd", probabilities, memory[..., head_dim:], preferred_element_type=jnp.float32
    ).astype(jnp.bfloat16)
    ctx_all = lax.all_gather(context, "ingest", axis=0, tiled=False)
    row_count = utterances * frame_span
    attn = grouped_terms(
        ctx_all.reshape(groups, row_count, head_dim),
        w_out_full.reshape(groups, head_dim, model_width),
    )
    residual = x_rows.reshape(row_count, model_width) + attn
    normed2 = normalize(residual, ln2_gain)
    mixed = jnp.dot(
        normed2, w_pw1.reshape(model_width, 2 * local_width), preferred_element_type=jnp.float32
    )
    glu_out = (mixed[:, :local_width] * jax.nn.sigmoid(mixed[:, local_width:])).astype(jnp.bfloat16)
    glu_out = glu_out.reshape(utterances, frame_span, local_width)
    joined = jnp.concatenate([conv_state, glu_out], axis=1)
    joined_f = joined.astype(jnp.float32)
    running = jnp.zeros((utterances, frame_span, local_width), jnp.float32)
    for tap_index in range(taps):
        running = running + joined_f[:, tap_index : tap_index + frame_span, :] * dw_weight[
            tap_index
        ].astype(jnp.float32)
    activated = jax.nn.silu(running * bn_scale + bn_shift).astype(jnp.bfloat16)
    act_all = lax.all_gather(activated, "ingest", axis=0, tiled=False)
    conv_terms = grouped_terms(act_all.reshape(groups, row_count, local_width), w_pw2_cols)
    residual_own = lax.dynamic_slice_in_dim(residual, me * local_width, local_width, 1)
    result = (residual_own + conv_terms).reshape(utterances, frame_span, local_width)
    live_rows = frame_index[None, :] < frames[:, None]
    layer_out = jnp.where(live_rows[:, :, None], result, 0.0).astype(jnp.bfloat16)
    keep = jnp.arange(cache_len, dtype=jnp.int32)
    kv_pick = position[None, None, :] == keep[None, :, None] + frames[:, None, None]
    kv_next = jnp.einsum(
        "srp,spd->srd", kv_pick.astype(jnp.bfloat16), memory, preferred_element_type=jnp.float32
    ).astype(jnp.bfloat16)
    conv_keep = jnp.arange(conv_len, dtype=jnp.int32)
    conv_pos = jnp.arange(joined.shape[1], dtype=jnp.int32)
    conv_pick = conv_pos[None, None, :] == conv_keep[None, :, None] + frames[:, None, None]
    conv_next = jnp.einsum(
        "srp,spd->srd", conv_pick.astype(jnp.bfloat16), joined, preferred_element_type=jnp.float32
    ).astype(jnp.bfloat16)
    return (layer_out, kv_next.reshape(kv_cache.shape), conv_next)


def solution(mesh):
    in_specs = (
        P("owner", None, "ingest"),
        P("owner"),
        P("owner"),
        P("owner"),
        P("owner", "ingest", None, None),
        P("owner", None, "ingest"),
        P("owner"),
        P(),
        P(None, "ingest", None),
        P("ingest", None),
        P(),
        P(None, None, "ingest"),
        P(None, "ingest"),
        P("ingest"),
        P("ingest"),
        P("ingest", None),
    )
    out_specs = (
        P("owner", None, "ingest"),
        P("owner", "ingest", None, None),
        P("owner", None, "ingest"),
    )
    return jax.shard_map(shards, mesh=mesh, in_specs=in_specs, out_specs=out_specs, check_vma=False)
```

profile of v0, /device:TPU:1, one launch (start us, length us, event | category | flops | bytes accessed | tf_op | source)
XLA Modules:
  0.0 387.9 jit_solution(17638379592714041639)
XLA Ops:
  7.3 1.5 slice-done
  9.7 0.8 convolution_convert_fusion
  10.5 1.8 maximum_bitcast_fusion
  12.8 5.4 %reduce.8 = bf16[64,22784]{1,0:T(8,128)(2,1)} reduce(bf16[64,1,22784]{2,0,1:T(8,128)(2,1)} %maximum_bitcast_fusion, bf16[]{:T(256)} %broadcast.254), dimensions={1}, to_apply=%copy.30.reduce_sub_computation | reduce | bytes 5832706 | tf_op jit(solution)/shard_map/all_to_all | solution.py:90
  18.2 4.4 %reshape.407 = bf16[64,2,11392]{2,1,0:T(2,128)(2,1)} reshape(bf16[64,22784]{1,0:T(8,128)(2,1)} %reduce.8) | data formatting | bytes 5832704
  22.6 19.3 %all-to-all-start = ((bf16[64,2,11392]{2,1,0:T(2,128)(2,1)}), bf16[64,2,11392]{2,1,0:T(2,128)(2,1)}, u32[]{:S(2)}, u32[]{:S(2)}) async-start(bf16[64,2,11392]{2,1,0:T(2,128)(2,1)} %reshape.407), calls=%async_computation | async-start | bytes 5832704 | tf_op jit(solution)/shard_map/all_to_all | solution.py:90
  42.0 127.4 %all-to-all-done = bf16[64,2,11392]{2,1,0:T(2,128)(2,1)} async-done(((bf16[64,2,11392]{2,1,0:T(2,128)(2,1)}), bf16[64,2,11392]{2,1,0:T(2,128)(2,1)}, u32[]{:S(2)}, u32[]{:S(2)}) %all-to-all-start) | async-done | bytes 2916384 | tf_op jit(solution)/shard_map/all_to_all | solution.py:90
  169.5 16.8 %reshape.408 = bf16[64,1,22784]{2,1,0:T(2,128)(2,1)} reshape(bf16[64,2,11392]{2,1,0:T(2,128)(2,1)} %all-to-all-done) | data formatting | bytes 5832704
  186.2 3.1 copy.57
  189.4 1.5 copy-done.3
  191.2 0.9 all_gather_reshape.3
  192.5 2.2 convolution_convert_fusion.1
  194.7 1.2 slice.143
  195.9 2.5 reshape.378
  198.4 26.5 %all-gather.7.cloned.1.call-done = bf16[8,33,28,128]{3,2,1,0:T(8,128)(2,1)} async-done(((bf16[1,33,28,128]{3,2,1,0:T(8,128)(2,1)}), bf16[8,33,28,128]{3,2,1,0:T(8,128)(2,1)}) %all-gather.7.cloned.1.call-update) | async-done | bytes 1892368 | tf_op jit(solution)/shard_map/all_gather | solution.py:119
  224.9 5.3 %bitcast_reduce_fusion = (f32[33,28]{1,0:T(8,128)S(1)}, f32[33,28]{1,0:T(8,128)S(1)}) fusion(bf16[8,33,28,128]{3,2,1,0:T(8,128)(2,1)} %all-gather.7.cloned.1.call-done), kind=kLoop, calls=%fused_computation.9 | loop fusion | flops 3782856 | bytes 1899744 | tf_op jit(solution)/shard_map/reduce_sum | solution.py:12
  230.3 5.5 %fusion.3 = bf16[33,28,8,128]{3,2,1,0:T(8,128)(2,1)} fusion(f32[8,128]{1,0:T(8,128)S(1)} %bitcast.128, f32[33,28]{1,0:T(8,128)S(1)} %get-tuple-element.24, f32[33,28]{1,0:T(8,128)S(1)} %get-tuple-element.23, bf16[8,33,28,128]{3,2,1,0:T(8,128)(2,1)S(1)} %copy-done.2), kind=kLoop, calls=%fused_computation.13 | loop fusion | flops 4730880 | bytes 3796192 | tf_op jit(solution)/shard_map/convert_element_type | solution.py:14
  235.7 4.1 %convert_element_type.219 = bf16[33,28,1024]{2,1,0:T(8,128)(2,1)} reshape(bf16[33,28,8,128]{3,2,1,0:T(8,128)(2,1)} %fusion.3) | data formatting | bytes 3784704 | tf_op jit(solution)/shard_map/convert_element_type | solution.py:14
  239.9 3.0 convolution_convert_fusion.5
  243.3 1.2 copy-done.9
  244.5 0.6 fusion.10
  245.5 3.8 convolution_convert_fusion.6
  249.3 0.7 all-gather.9.cloned.1.call-update
  250.9 0.8 slice_bitcast_fusion
  251.8 31.2 %all-gather.11.cloned.1.call-done = bf16[264,28,128]{2,1,0:T(8,128)(2,1)} async-done(((bf16[33,28,128]{2,1,0:T(8,128)(2,1)}), bf16[264,28,128]{2,1,0:T(8,128)(2,1)}) %all-gather.11.cloned.1.call-update) | async-done | bytes 1892368 | tf_op jit(solution)/shard_map/all_gather | solution.py:148
  283.0 3.6 reshape.379
  286.6 32.0 %all-gather.9.cloned.1.call-done = bf16[1024,1024]{1,0:T(8,128)(2,1)} async-done(((bf16[128,1024]{1,0:T(8,128)(2,1)}), bf16[1024,1024]{1,0:T(8,128)(2,1)}) %all-gather.9.cloned.1.call-update) | async-done | bytes 2097168 | tf_op jit(solution)/shard_map/all_gather | solution.py:61
  318.6 6.6 %convert_reduce_fusion = f32[924,1024]{1,0:T(8,128)S(1)} fusion(bf16[8,924,128]{2,1,0:T(8,128)(2,1)} %reshape.379, bf16[8,128,1024]{2,1,0:T(8,128)(2,1)} %bitcast.129), kind=kOutput, calls=%fused_computation.1 | convolution fusion | flops 1959530496 | bytes 7774208 | tf_op jit(solution)/shard_map/grc,gcn->grn/dot_general | solution.py:24
  325.3 0.9 copy.41
  326.2 1.0 copy-done.5
  327.5 3.6 fusion.6
  331.1 5.0 %multiply_convert_fusion = bf16[33,28,8,128]{3,2,1,0:T(8,128)(2,1)S(1)} fusion(f32[8,128]{1,0:T(8,128)S(1)} %bitcast.127, f32[33,28]{1,0:T(8,128)S(1)} %get-tuple-element.22, f32[33,28]{1,0:T(8,128)S(1)} %get-tuple-element.21, f32[33,28,8,128]{3,2,1,0:T(8,128)S(1)} %bitcast.106, bf16[8,33,28,128]{3,2,1,0:T(8,128)(2,1)S(1)} %copy-done.2), kind=kLoop, calls=%fused_computation.15 | loop fusion | flops 5677056 | bytes 7580896 | tf_op jit(solution)/shard_map/convert_element_type | solution.py:14
  337.3 0.7 fusion.31
  338.2 0.7 reshape.383
  338.9 1.0 fusion.46
  340.0 1.4 multiply_convert_fusion.1
  341.4 1.1 copy.32
  342.5 0.9 copy.33
  343.4 4.3 %all-to-all-start.1 = ((bf16[8,128,128]{2,1,0:T(8,128)(2,1)}), bf16[8,128,128]{2,1,0:T(8,128)(2,1)}, u32[]{:S(2)}, u32[]{:S(2)}) async-start(bf16[8,128,128]{2,1,0:T(8,128)(2,1)} %bitcast.18), calls=%async_computation.1 | async-start | bytes 524288 | tf_op jit(solution)/shard_map/all_to_all | solution.py:62
  347.9 0.9 copy_convert_fusion
  349.2 1.9 fusion.7
  351.4 2.8 copy.39
  354.1 0.9 convolution_convert_fusion.7
  355.0 19.9 %all-gather.13.cloned.1.call-done = bf16[264,28,128]{2,1,0:T(8,128)(2,1)} async-done(((bf16[33,28,128]{2,1,0:T(8,128)(2,1)}), bf16[264,28,128]{2,1,0:T(8,128)(2,1)}) %all-gather.13.cloned.1.call-update) | async-done | bytes 1892368 | tf_op jit(solution)/shard_map/all_gather | solution.py:169
  374.9 2.5 reshape.384
  377.5 1.6 convert_reduce_fusion.1
  379.1 1.3 fusion.38
  380.4 0.9 select_convert_fusion
  (97 shorter events, 6.5 us)
Async XLA Ops:
  7.2 232.7 %copy-start = (bf16[1024,1,384]{2,0,1:T(8,128)(2,1)S(1)}, bf16[1024,1,384]{2,0,1:T(8,128)(2,1)}, u32[]{:S(2)}) copy-start(bf16[1024,1,384]{2,0,1:T(8,128)(2,1)} %param.24) | copy-start | bytes 2359300
  7.2 1.6 slice-start
  7.2 1.9 slice-start.1
  7.2 1.9 copy-start.11
  7.2 2.0 copy-start.26
  7.2 2.1 copy-start.23
  7.3 2.5 copy-start.24
  22.6 146.9 %all-to-all-start = ((bf16[64,2,11392]{2,1,0:T(2,128)(2,1)}), bf16[64,2,11392]{2,1,0:T(2,128)(2,1)}, u32[]{:S(2)}, u32[]{:S(2)}) async-start(bf16[64,2,11392]{2,1,0:T(2,128)(2,1)} %reshape.407), calls=%async_computation | async-start | bytes 5832704 | tf_op jit(solution)/shard_map/all_to_all | solution.py:90
  42.0 182.9 %all-gather.7.cloned.1.call-start = ((), (), s32[]{:S(2)}) async-start(), calls=%async_computation.2 | async-start | bytes 2433024 | tf_op jit(solution)/shard_map/all_gather | solution.py:119
  186.2 6.2 %copy-start.13 = (s32[33]{0:T(128)S(1)}, s32[33]{0:T(128)}, u32[]{:S(2)}) copy-start(s32[33]{0:T(128)} %param.19) | copy-start | bytes 400
  186.2 6.2 %copy-start.8 = (bf16[33,1,70,256]{3,2,1,0:T(8,128)(2,1)S(1)}, bf16[33,1,70,256]{3,2,1,0:T(8,128)(2,1)}, u32[]{:S(2)}) copy-start(bf16[33,1,70,256]{3,2,1,0:T(8,128)(2,1)} %param.20) | copy-start | bytes 3548164
  189.3 1.6 copy-start.3
  192.1 90.9 %all-gather.11.cloned.1.call-start = ((), (), s32[]{:S(2)}) async-start(), calls=%async_computation.4 | async-start | bytes 2433024 | tf_op jit(solution)/shard_map/all_gather | solution.py:148
  194.7 3.7 copy-start.4
  195.9 34.4 %copy-start.16 = (f32[1024]{0:T(1024)S(1)}, f32[1024]{0:T(1024)}, u32[]{:S(2)}) copy-start(f32[1024]{0:T(1024)} %param.23) | copy-start | bytes 12292
  224.9 5.4 %copy-start.2 = (bf16[8,33,28,128]{3,2,1,0:T(8,128)(2,1)S(1)}, bf16[8,33,28,128]{3,2,1,0:T(8,128)(2,1)}, u32[]{:S(2)}) copy-start(bf16[8,33,28,128]{3,2,1,0:T(8,128)(2,1)} %all-gather.7.cloned.1.call-done) | copy-start | bytes 5677060
  239.9 3.1 copy-start.6
  243.3 1.2 copy-start.9
  245.1 5.2 %copy-start.12 = (bf16[33,8,128]{2,1,0:T(8,128)(2,1)S(1)}, bf16[33,8,128]{2,1,0:T(8,128)(2,1)}, u32[]{:S(2)}) copy-start(bf16[33,8,128]{2,1,0:T(8,128)(2,1)} %param.21) | copy-start | bytes 202756
  245.1 5.2 %copy-start.14 = (bf16[9,128]{1,0:T(8,128)(2,1)S(1)}, bf16[9,128]{1,0:T(8,128)(2,1)}, u32[]{:S(2)}) copy-start(bf16[9,128]{1,0:T(8,128)(2,1)} %param.28) | copy-start | bytes 6916
  249.3 69.4 %all-gather.9.cloned.1.call-start = ((), (), s32[]{:S(2)}) async-start(), calls=%async_computation.3 | async-start | bytes 2359296 | tf_op jit(solution)/shard_map/all_gather | solution.py:61
  250.0 124.9 %all-gather.13.cloned.1.call-start = ((), (), s32[]{:S(2)}) async-start(), calls=%async_computation.5 | async-start | bytes 2433024 | tf_op jit(solution)/shard_map/all_gather | solution.py:169
  325.3 1.9 copy-start.5
  327.4 3.6 copy-start.15
  336.3 1.0 copy-start.25
  338.0 2.0 copy-start.17
  338.0 2.0 copy-start.18
  338.0 2.0 copy-start.19
  338.0 2.0 copy-start.20
  338.0 2.0 copy-start.21
  338.0 2.0 copy-start.22
  343.4 34.0 %all-to-all-start.1 = ((bf16[8,128,128]{2,1,0:T(8,128)(2,1)}), bf16[8,128,128]{2,1,0:T(8,128)(2,1)}, u32[]{:S(2)}, u32[]{:S(2)}) async-start(bf16[8,128,128]{2,1,0:T(8,128)(2,1)} %bitcast.18), calls=%async_computation.1 | async-start | bytes 524288 | tf_op jit(solution)/shard_map/all_to_all | solution.py:62
  347.9 1.3 copy-start.7
  351.3 2.8 copy-start.10
  374.9 6.4 %copy-start.1 = (bf16[1024,1,384]{2,0,1:T(8,128)(2,1)S(1)}, bf16[1024,1,384]{2,0,1:T(8,128)(2,1)}, u32[]{:S(2)}) copy-start(bf16[1024,1,384]{2,0,1:T(8,128)(2,1)} %param.24) | copy-start | bytes 2359300
Sparse Core Ops, SparseCore 0:
  192.2 32.6 all-gather.6
  249.4 33.5 all-gather.10
  285.2 33.4 all-gather.8
  341.5 33.3 all-gather.12
where the time goes:
time: 389 us; the launch traced here: 388 us
  waiting for transfers between devices  238 us (61%)
  local copies, waits for them, and re-layouts  54.9 us (14%)
  other arithmetic  34 us (9%)
  starting transfers between devices  24.2 us (6%)
  matrix products  22.6 us (6%)
  between operations  14.4 us (4%)
    all_to_all x1, waiting for transfers between devices, shards(): lax.all_to_all(jnp.concatenate([frame_send, cache_send], axis=1), 'owner'...  127 us
    unnamed x70, local copies, waits for them, and re-layouts  36.2 us
    all_gather x1, waiting for transfers between devices, shards(): w_out_full = lax.all_gather(w_out, 'ingest', axis=0, tiled=True)  32 us
    all_gather x1, waiting for transfers between devices, shards(): ctx_all = lax.all_gather(context, 'ingest', axis=0, tiled=False)  31.2 us
    all_gather x1, waiting for transfers between devices, shards(): x_all = lax.all_gather(arranged, 'ingest', axis=0, tiled=False)  26.5 us
    all_gather x1, waiting for transfers between devices, shards(): act_all = lax.all_gather(activated, 'ingest', axis=0, tiled=False)  19.9 us
    all_to_all x1, starting transfers between devices, shards(): lax.all_to_all(jnp.concatenate([frame_send, cache_send], axis=1), 'owner'...  19.3 us
    convert_element_type x2, other arithmetic, normalize(): ((values - row_mean) * lax.rsqrt(spread + norm_eps) * gain_cols).astype(j...  10.5 us
  transfers between devices with their start and end apart: 6, of which 5 were waited for; matrix products, arithmetic and copies ran while one was open for 6% of the time, Pallas kernels for 0%

commit v1 on v0

--- a/solution.py
+++ b/solution.py
@@ -58,7 +58,19 @@
     moving = mig_owner.shape[0]
     settled = utterances - moving
     lanes = 128
-    w_out_full = lax.all_gather(w_out, "ingest", axis=0, tiled=True)
+
+    def _cover_column(t0):
+        n_lanes = lax.axis_size("ingest")
+        mid_arr = [(k0 - 1, k0) for k0 in range(1, n_lanes)] + [(n_lanes - 1, 0)]
+        carry_in = t0
+        history = [carry_in]
+        for _ in [*range(n_lanes - 1)]:
+            carry_in = lax.ppermute(carry_in, "ingest", mid_arr)
+            history += [carry_in]
+        w1 = jnp.concatenate([*reversed(history)], axis=0)
+        return jnp.roll(w1, (lax.axis_index("ingest") + 1) * carry_in.shape[0], axis=0)
+
+    w_out_full = _cover_column(w_out)
     w_pw2_cols = lax.all_to_all(
         w_pw2.reshape(local_width, groups, local_width).transpose(1, 0, 2),
         "ingest",

time: 389 us -> 362 us (0.931)
  waiting for transfers between devices: 238 us -> 170 us
  starting transfers between devices: 24.2 us -> 51 us
  local copies, waits for them, and re-layouts: 54.9 us -> 67.4 us
    all_gather x1 -> x0, waiting for transfers between devices: 32 us -> none  [shards(): w_out_full = lax.all_gather(w_out, 'ingest', axis=0, tiled=True)]
    all_gather x1, waiting for transfers between devices: 31.2 us -> 1.87 us  [shards(): ctx_all = lax.all_gather(context, 'ingest', axis=0, tiled=False)]
    ppermute x0 -> x7, waiting for transfers between devices: none -> 28.8 us  [_cover_column(): carry_in = lax.ppermute(carry_in, 'ingest', mid_arr)]
    all_gather x1, waiting for transfers between devices: 26.5 us -> 0.01 us  [shards(): x_all = lax.all_gather(arranged, 'ingest', axis=0, tiled=False)]
    ppermute x0 -> x7, starting transfers between devices: none -> 17.6 us  [_cover_column(): carry_in = lax.ppermute(carry_in, 'ingest', mid_arr)]
    unnamed x70 -> x105, local copies, waits for them, and re-layouts: 36.2 us -> 46.4 us
    all_to_all x1, starting transfers between devices: 4.26 us -> 13.7 us  [shards(): lax.all_to_all(w_pw2.reshape(local_width, groups, local_width).transpose(...]
    all_gather x1, waiting for transfers between devices: 19.9 us -> 11.7 us  [shards(): act_all = lax.all_gather(activated, 'ingest', axis=0, tiled=False)]
  transfers between devices with their start and end apart: 6 -> 12, of which waited for: 5 -> 9; matrix products, arithmetic and copies ran while one was open for 6% -> 15% of each run, Pallas kernels for 0% -> 0%
where the time goes in v1:
time: 362 us; the launch traced here: 360 us
  waiting for transfers between devices  170 us (47%)
  local copies, waits for them, and re-layouts  67.4 us (19%)
  starting transfers between devices  51 us (14%)
  other arithmetic  34.6 us (10%)
  matrix products  23 us (6%)
  between operations  14.5 us (4%)
    all_to_all x1, waiting for transfers between devices, shards(): lax.all_to_all(jnp.concatenate([frame_send, cache_send], axis=1), 'owner'...  127 us
    unnamed x105, local copies, waits for them, and re-layouts  46.4 us
    ppermute x7, waiting for transfers between devices, _cover_column(): carry_in = lax.ppermute(carry_in, 'ingest', mid_arr)  28.8 us
    all_to_all x1, starting transfers between devices, shards(): lax.all_to_all(jnp.concatenate([frame_send, cache_send], axis=1), 'owner'...  19.3 us
    ppermute x7, starting transfers between devices, _cover_column(): carry_in = lax.ppermute(carry_in, 'ingest', mid_arr)  17.6 us
    all_to_all x1, starting transfers between devices, shards(): lax.all_to_all(w_pw2.reshape(local_width, groups, local_width).transpose(...  13.7 us
    all_gather x1, waiting for transfers between devices, shards(): act_all = lax.all_gather(activated, 'ingest', axis=0, tiled=False)  11.7 us
    convert_element_type x2, other arithmetic, normalize(): ((values - row_mean) * lax.rsqrt(spread + norm_eps) * gain_cols).astype(j...  10.5 us
  transfers between devices with their start and end apart: 12, of which 9 were waited for; matrix products, arithmetic and copies ran while one was open for 15% of the time, Pallas kernels for 0%

profile of v1, /device:TPU:1, one launch (start us, length us, event | category | flops | bytes accessed | tf_op | source)
XLA Modules:
  0.0 360.3 jit_solution(15492153064072090615)
XLA Ops:
  7.3 1.5 slice-done
  10.5 1.8 maximum_bitcast_fusion
  12.8 5.4 %reduce.8 = bf16[64,22784]{1,0:T(8,128)(2,1)} reduce(bf16[64,1,22784]{2,0,1:T(8,128)(2,1)} %maximum_bitcast_fusion, bf16[]{:T(256)} %broadcast.255), dimensions={1}, to_apply=%copy.30.reduce_sub_computation | reduce | bytes 5832706 | tf_op jit(solution)/shard_map/all_to_all | solution.py:102
  18.2 4.4 %reshape.407 = bf16[64,2,11392]{2,1,0:T(2,128)(2,1)} reshape(bf16[64,22784]{1,0:T(8,128)(2,1)} %reduce.8) | data formatting | bytes 5832704
  22.6 19.3 %all-to-all-start = ((bf16[64,2,11392]{2,1,0:T(2,128)(2,1)}), bf16[64,2,11392]{2,1,0:T(2,128)(2,1)}, u32[]{:S(2)}, u32[]{:S(2)}) async-start(bf16[64,2,11392]{2,1,0:T(2,128)(2,1)} %reshape.407), calls=%async_computation | async-start | bytes 5832704 | tf_op jit(solution)/shard_map/all_to_all | solution.py:102
  42.0 127.4 %all-to-all-done = bf16[64,2,11392]{2,1,0:T(2,128)(2,1)} async-done(((bf16[64,2,11392]{2,1,0:T(2,128)(2,1)}), bf16[64,2,11392]{2,1,0:T(2,128)(2,1)}, u32[]{:S(2)}, u32[]{:S(2)}) %all-to-all-start) | async-done | bytes 2916384 | tf_op jit(solution)/shard_map/all_to_all | solution.py:102
  169.5 16.7 %reshape.408 = bf16[64,1,22784]{2,1,0:T(2,128)(2,1)} reshape(bf16[64,2,11392]{2,1,0:T(2,128)(2,1)} %all-to-all-done) | data formatting | bytes 5832704
  186.2 3.1 copy.57
  189.4 1.5 copy-done.3
  192.3 8.3 %collective-permute-start = (bf16[128,1024]{1,0:T(8,128)(2,1)S(1)}, bf16[128,1024]{1,0:T(8,128)(2,1)S(1)}, u32[]{:S(2)}, u32[]{:S(2)}) collective-permute-start(bf16[128,1024]{1,0:T(8,128)(2,1)S(1)} %copy-done.11), channel_id=1, source_target_pairs={{0,64},{64,128},{128,192},{192,256},{256,320},{320,384},{384,448},... | collective-permute-start | bytes 786440 | tf_op jit(solution)/shard_map/ppermute | solution.py:68
  200.6 3.3 collective-permute-done
  203.9 2.5 collective-permute-start.1
  207.2 2.8 collective-permute-done.1
  210.0 2.5 collective-permute-start.2
  212.5 5.5 %collective-permute-done.2 = bf16[128,1024]{1,0:T(8,128)(2,1)} collective-permute-done((bf16[128,1024]{1,0:T(8,128)(2,1)S(1)}, bf16[128,1024]{1,0:T(8,128)(2,1)}, u32[]{:S(2)}, u32[]{:S(2)}) %collective-permute-start.2) | collective-permute-done | bytes 262176 | tf_op jit(solution)/shard_map/ppermute | solution.py:68
  217.9 2.6 collective-permute-start.3
  220.5 2.2 convolution_convert_fusion.1
  222.8 1.2 slice.143
  224.0 2.5 reshape.378
  226.5 5.3 %bitcast_reduce_fusion = (f32[33,28]{1,0:T(8,128)S(1)}, f32[33,28]{1,0:T(8,128)S(1)}) fusion(bf16[8,33,28,128]{3,2,1,0:T(8,128)(2,1)} %all-gather.6.cloned.1.call-done), kind=kLoop, calls=%fused_computation.9 | loop fusion | flops 3782856 | bytes 1899744 | tf_op jit(solution)/shard_map/reduce_sum | solution.py:12
  231.9 5.5 %fusion.3 = bf16[33,28,8,128]{3,2,1,0:T(8,128)(2,1)} fusion(f32[8,128]{1,0:T(8,128)S(1)} %bitcast.129, f32[33,28]{1,0:T(8,128)S(1)} %get-tuple-element.24, f32[33,28]{1,0:T(8,128)S(1)} %get-tuple-element.23, bf16[8,33,28,128]{3,2,1,0:T(8,128)(2,1)S(1)} %copy-done.2), kind=kLoop, calls=%fused_computation.13 | loop fusion | flops 4730880 | bytes 3796192 | tf_op jit(solution)/shard_map/convert_element_type | solution.py:14
  237.4 4.1 %convert_element_type.219 = bf16[33,28,1024]{2,1,0:T(8,128)(2,1)} reshape(bf16[33,28,8,128]{3,2,1,0:T(8,128)(2,1)} %fusion.3) | data formatting | bytes 3784704 | tf_op jit(solution)/shard_map/convert_element_type | solution.py:14
  241.5 3.0 convolution_convert_fusion.5
  244.9 1.2 copy-done.9
  247.9 4.2 %convolution_convert_fusion.6 = bf16[33,28,128]{2,1,0:T(8,128)(2,1)} fusion(bf16[33,98,256]{2,1,0:T(8,128)(2,1)} %copy-done.9, f32[33,28]{1,0:T(8,128)S(1)} %fusion.61, f32[33,28,98]{2,1,0:T(8,128)} %copy-done.19), kind=kOutput, calls=%fused_computation.35 | convolution fusion | flops 23572260 | bytes 2200176 | tf_op jit(solution)/shard_map/sqk,skd->sqd/dot_general | solution.py:157
  253.0 5.0 %collective-permute-done.4 = bf16[128,1024]{1,0:T(8,128)(2,1)S(1)} collective-permute-done((bf16[128,1024]{1,0:T(8,128)(2,1)}, bf16[128,1024]{1,0:T(8,128)(2,1)S(1)}, u32[]{:S(2)}, u32[]{:S(2)}) %collective-permute-start.4) | collective-permute-done | bytes 262176 | tf_op jit(solution)/shard_map/ppermute | solution.py:68
  258.7 1.0 collective-permute-start.5
  259.7 6.2 %collective-permute-done.5 = bf16[128,1024]{1,0:T(8,128)(2,1)} collective-permute-done((bf16[128,1024]{1,0:T(8,128)(2,1)S(1)}, bf16[128,1024]{1,0:T(8,128)(2,1)}, u32[]{:S(2)}, u32[]{:S(2)}) %collective-permute-start.5) | collective-permute-done | bytes 262176 | tf_op jit(solution)/shard_map/ppermute | solution.py:68
  267.1 6.0 %collective-permute-done.6 = bf16[128,1024]{1,0:T(8,128)(2,1)} collective-permute-done((bf16[128,1024]{1,0:T(8,128)(2,1)}, bf16[128,1024]{1,0:T(8,128)(2,1)}, u32[]{:S(2)}, u32[]{:S(2)}) %collective-permute-start.6) | collective-permute-done | bytes 262176 | tf_op jit(solution)/shard_map/ppermute | solution.py:68
  275.1 1.0 constant_dynamic-update-slice_fusion.13
  280.1 1.0 constant_dynamic-update-slice_fusion.4
  282.1 1.5 constant_dynamic-slice_fusion
  284.5 1.9 all-gather.8.cloned.1.call-done
  286.4 3.7 %reshape.379 = bf16[8,924,128]{2,1,0:T(8,128)(2,1)} reshape(bf16[264,28,128]{2,1,0:T(8,128)(2,1)} %all-gather.8.cloned.1.call-done) | data formatting | bytes 3784704 | tf_op jit(solution)/shard_map/reshape | solution.py:163
  290.0 6.6 %convert_reduce_fusion = f32[924,1024]{1,0:T(8,128)S(1)} fusion(bf16[8,924,128]{2,1,0:T(8,128)(2,1)} %reshape.379, bf16[8,128,1024]{2,1,0:T(8,128)(2,1)} %bitcast.119), kind=kOutput, calls=%fused_computation.1 | convolution fusion | flops 1959530496 | bytes 7774208 | tf_op jit(solution)/shard_map/grc,gcn->grn/dot_general | solution.py:24
  297.6 1.0 copy-done.5
  298.8 3.6 fusion.6
  302.5 5.0 %multiply_convert_fusion = bf16[33,28,8,128]{3,2,1,0:T(8,128)(2,1)S(1)} fusion(f32[8,128]{1,0:T(8,128)S(1)} %bitcast.128, f32[33,28]{1,0:T(8,128)S(1)} %get-tuple-element.22, f32[33,28]{1,0:T(8,128)S(1)} %get-tuple-element.21, f32[33,28,8,128]{3,2,1,0:T(8,128)S(1)} %bitcast.106, bf16[8,33,28,128]{3,2,1,0:T(8,128)(2,1)S(1)} %copy-done.2), kind=kLoop, calls=%fused_computation.15 | loop fusion | flops 5677056 | bytes 7580896 | tf_op jit(solution)/shard_map/convert_element_type | solution.py:14
  310.2 1.0 fusion.46
  311.2 1.4 multiply_convert_fusion.1
  312.7 1.1 copy.32
  314.6 13.7 %all-to-all-start.1 = ((bf16[8,128,128]{2,1,0:T(8,128)(2,1)}), bf16[8,128,128]{2,1,0:T(8,128)(2,1)}, u32[]{:S(2)}, u32[]{:S(2)}) async-start(bf16[8,128,128]{2,1,0:T(8,128)(2,1)} %bitcast.18), calls=%async_computation.1 | async-start | bytes 524288 | tf_op jit(solution)/shard_map/all_to_all | solution.py:74
  329.9 1.9 fusion.7
  332.0 2.7 copy.39
  335.7 11.7 %all-gather.10.cloned.1.call-done = bf16[264,28,128]{2,1,0:T(8,128)(2,1)} async-done(((bf16[33,28,128]{2,1,0:T(8,128)(2,1)}), bf16[264,28,128]{2,1,0:T(8,128)(2,1)}) %all-gather.10.cloned.1.call-update) | async-done | bytes 1892368 | tf_op jit(solution)/shard_map/all_gather | solution.py:181
  347.4 2.5 reshape.384
  350.0 1.6 convert_reduce_fusion.1
  351.6 1.3 fusion.38
  (145 shorter events, 25.6 us)
Async XLA Ops:
  7.2 234.3 %copy-start = (bf16[1024,1,384]{2,0,1:T(8,128)(2,1)S(1)}, bf16[1024,1,384]{2,0,1:T(8,128)(2,1)}, u32[]{:S(2)}) copy-start(bf16[1024,1,384]{2,0,1:T(8,128)(2,1)} %param.24) | copy-start | bytes 2359300
  7.2 1.6 slice-start
  7.2 1.9 slice-start.1
  7.2 1.9 copy-start.20
  7.2 2.0 copy-start.36
  7.2 2.1 copy-start.33
  7.3 2.5 copy-start.34
  22.6 146.9 %all-to-all-start = ((bf16[64,2,11392]{2,1,0:T(2,128)(2,1)}), bf16[64,2,11392]{2,1,0:T(2,128)(2,1)}, u32[]{:S(2)}, u32[]{:S(2)}) async-start(bf16[64,2,11392]{2,1,0:T(2,128)(2,1)} %reshape.407), calls=%async_computation | async-start | bytes 5832704 | tf_op jit(solution)/shard_map/all_to_all | solution.py:102
  42.0 184.5 %all-gather.6.cloned.1.call-start = ((), (), s32[]{:S(2)}) async-start(), calls=%async_computation.2 | async-start | bytes 2433024 | tf_op jit(solution)/shard_map/all_gather | solution.py:131
  186.2 6.1 %copy-start.11 = (bf16[128,1024]{1,0:T(8,128)(2,1)S(1)}, bf16[128,1024]{1,0:T(8,128)(2,1)}, u32[]{:S(2)}) copy-start(bf16[128,1024]{1,0:T(8,128)(2,1)} %param.25) | copy-start | bytes 786436
  186.2 20.9 %copy-start.21 = (s32[33]{0:T(128)S(1)}, s32[33]{0:T(128)}, u32[]{:S(2)}) copy-start(s32[33]{0:T(128)} %param.19) | copy-start | bytes 400
  186.2 26.3 %copy-start.8 = (bf16[33,1,70,256]{3,2,1,0:T(8,128)(2,1)S(1)}, bf16[33,1,70,256]{3,2,1,0:T(8,128)(2,1)}, u32[]{:S(2)}) copy-start(bf16[33,1,70,256]{3,2,1,0:T(8,128)(2,1)} %param.20) | copy-start | bytes 3548164
  189.3 1.6 copy-start.3
  192.0 94.3 %all-gather.8.cloned.1.call-start = ((), (), s32[]{:S(2)}) async-start(), calls=%async_computation.3 | async-start | bytes 2433024 | tf_op jit(solution)/shard_map/all_gather | solution.py:160
  192.3 11.7 %collective-permute-start = (bf16[128,1024]{1,0:T(8,128)(2,1)S(1)}, bf16[128,1024]{1,0:T(8,128)(2,1)S(1)}, u32[]{:S(2)}, u32[]{:S(2)}) collective-permute-start(bf16[128,1024]{1,0:T(8,128)(2,1)S(1)} %copy-done.11), channel_id=1, source_target_pairs={{0,64},{64,128},{128,192},{192,256},{256,320},{320,384},{384,448},... | collective-permute-start | bytes 786440 | tf_op jit(solution)/shard_map/ppermute | solution.py:68
  203.9 20.1 %copy-start.13 = (bf16[128,1024]{1,0:T(8,128)(2,1)}, bf16[128,1024]{1,0:T(8,128)(2,1)S(1)}, u32[]{:S(2)}) copy-start(bf16[128,1024]{1,0:T(8,128)(2,1)S(1)} %collective-permute-done) | copy-start | bytes 786436
  203.9 6.0 %collective-permute-start.1 = (bf16[128,1024]{1,0:T(8,128)(2,1)S(1)}, bf16[128,1024]{1,0:T(8,128)(2,1)S(1)}, u32[]{:S(2)}, u32[]{:S(2)}) collective-permute-start(bf16[128,1024]{1,0:T(8,128)(2,1)S(1)} %collective-permute-done), channel_id=1, source_target_pairs={{0,64},{64,128},{128,192},{192,256},{256,320},{320,384},{384,448},... | collective-permute-start | bytes 786440 | tf_op jit(solution)/shard_map/ppermute | solution.py:68
  210.0 14.0 %copy-start.15 = (bf16[128,1024]{1,0:T(8,128)(2,1)}, bf16[128,1024]{1,0:T(8,128)(2,1)S(1)}, u32[]{:S(2)}) copy-start(bf16[128,1024]{1,0:T(8,128)(2,1)S(1)} %collective-permute-done.1) | copy-start | bytes 786436
  210.0 8.0 %collective-permute-start.2 = (bf16[128,1024]{1,0:T(8,128)(2,1)S(1)}, bf16[128,1024]{1,0:T(8,128)(2,1)}, u32[]{:S(2)}, u32[]{:S(2)}) collective-permute-start(bf16[128,1024]{1,0:T(8,128)(2,1)S(1)} %collective-permute-done.1), channel_id=1, source_target_pairs={{0,64},{64,128},{128,192},{192,256},{256,320},{320,384},{384,448},... | collective-permute-start | bytes 786440 | tf_op jit(solution)/shard_map/ppermute | solution.py:68
  217.9 34.2 %collective-permute-start.3 = (bf16[128,1024]{1,0:T(8,128)(2,1)}, bf16[128,1024]{1,0:T(8,128)(2,1)}, u32[]{:S(2)}, u32[]{:S(2)}) collective-permute-start(bf16[128,1024]{1,0:T(8,128)(2,1)} %collective-permute-done.2), channel_id=1, source_target_pairs={{0,64},{64,128},{128,192},{192,256},{256,320},{320,384},{384,448},... | collective-permute-start | bytes 786440 | tf_op jit(solution)/shard_map/ppermute | solution.py:68
  222.7 3.8 %copy-start.4 = (bf16[32,18944]{1,0:T(8,128)(2,1)}, bf16[32,18944]{1,0:T(8,128)(2,1)S(1)}, u32[]{:S(2)}) copy-start(bf16[32,18944]{1,0:T(8,128)(2,1)S(1)} %convolution_convert_fusion.1) | copy-start | bytes 3637252
  222.8 9.1 %copy-start.24 = (f32[1024]{0:T(1024)S(1)}, f32[1024]{0:T(1024)}, u32[]{:S(2)}) copy-start(f32[1024]{0:T(1024)} %param.23) | copy-start | bytes 12292
  226.5 5.4 %copy-start.2 = (bf16[8,33,28,128]{3,2,1,0:T(8,128)(2,1)S(1)}, bf16[8,33,28,128]{3,2,1,0:T(8,128)(2,1)}, u32[]{:S(2)}) copy-start(bf16[8,33,28,128]{3,2,1,0:T(8,128)(2,1)} %all-gather.6.cloned.1.call-done) | copy-start | bytes 5677060
  241.5 3.1 copy-start.6
  244.5 1.7 copy-start.25
  244.9 1.2 copy-start.9
  246.1 20.4 %copy-start.22 = (bf16[9,128]{1,0:T(8,128)(2,1)S(1)}, bf16[9,128]{1,0:T(8,128)(2,1)}, u32[]{:S(2)}) copy-start(bf16[9,128]{1,0:T(8,128)(2,1)} %param.28) | copy-start | bytes 6916
  247.9 30.1 %copy-start.16 = (bf16[128,1024]{1,0:T(8,128)(2,1)S(1)}, bf16[128,1024]{1,0:T(8,128)(2,1)}, u32[]{:S(2)}) copy-start(bf16[128,1024]{1,0:T(8,128)(2,1)} %copy-done.15) | copy-start | bytes 786436
  247.9 30.2 %copy-start.14 = (bf16[128,1024]{1,0:T(8,128)(2,1)S(1)}, bf16[128,1024]{1,0:T(8,128)(2,1)}, u32[]{:S(2)}) copy-start(bf16[128,1024]{1,0:T(8,128)(2,1)} %copy-done.13) | copy-start | bytes 786436
  247.9 30.2 %copy-start.12 = (bf16[128,1024]{1,0:T(8,128)(2,1)S(1)}, bf16[128,1024]{1,0:T(8,128)(2,1)}, u32[]{:S(2)}) copy-start(bf16[128,1024]{1,0:T(8,128)(2,1)} %param.25) | copy-start | bytes 786436
  252.1 95.3 %all-gather.10.cloned.1.call-start = ((), (), s32[]{:S(2)}) async-start(), calls=%async_computation.4 | async-start | bytes 2433024 | tf_op jit(solution)/shard_map/all_gather | solution.py:181
  252.2 5.8 %collective-permute-start.4 = (bf16[128,1024]{1,0:T(8,128)(2,1)}, bf16[128,1024]{1,0:T(8,128)(2,1)S(1)}, u32[]{:S(2)}, u32[]{:S(2)}) collective-permute-start(bf16[128,1024]{1,0:T(8,128)(2,1)} %collective-permute-done.3), channel_id=1, source_target_pairs={{0,64},{64,128},{128,192},{192,256},{256,320},{320,384},{384,448},... | collective-permute-start | bytes 786440 | tf_op jit(solution)/shard_map/ppermute | solution.py:68
  258.7 7.1 %collective-permute-start.5 = (bf16[128,1024]{1,0:T(8,128)(2,1)S(1)}, bf16[128,1024]{1,0:T(8,128)(2,1)}, u32[]{:S(2)}, u32[]{:S(2)}) collective-permute-start(bf16[128,1024]{1,0:T(8,128)(2,1)S(1)} %collective-permute-done.4), channel_id=1, source_target_pairs={{0,64},{64,128},{128,192},{192,256},{256,320},{320,384},{384,448},... | collective-permute-start | bytes 786440 | tf_op jit(solution)/shard_map/ppermute | solution.py:68
  265.8 7.3 %collective-permute-start.6 = (bf16[128,1024]{1,0:T(8,128)(2,1)}, bf16[128,1024]{1,0:T(8,128)(2,1)}, u32[]{:S(2)}, u32[]{:S(2)}) collective-permute-start(bf16[128,1024]{1,0:T(8,128)(2,1)} %collective-permute-done.5), channel_id=1, source_target_pairs={{0,64},{64,128},{128,192},{192,256},{256,320},{320,384},{384,448},... | collective-permute-start | bytes 786440 | tf_op jit(solution)/shard_map/ppermute | solution.py:68
  266.5 13.6 %copy-start.18 = (bf16[128,1024]{1,0:T(8,128)(2,1)S(1)}, bf16[128,1024]{1,0:T(8,128)(2,1)}, u32[]{:S(2)}) copy-start(bf16[128,1024]{1,0:T(8,128)(2,1)} %copy-done.17) | copy-start | bytes 786436
  296.6 1.9 copy-start.5
  298.8 3.6 %copy-start.23 = (f32[1024]{0:T(1024)S(1)}, f32[1024]{0:T(1024)}, u32[]{:S(2)}) copy-start(f32[1024]{0:T(1024)} %param.26) | copy-start | bytes 12292
  308.5 2.6 copy-start.26
  308.5 2.6 copy-start.27
  308.6 2.6 copy-start.28
  308.6 2.6 copy-start.29
  308.6 2.6 copy-start.30
  308.6 2.6 copy-start.31
  308.6 2.6 copy-start.32
  314.6 35.3 %all-to-all-start.1 = ((bf16[8,128,128]{2,1,0:T(8,128)(2,1)}), bf16[8,128,128]{2,1,0:T(8,128)(2,1)}, u32[]{:S(2)}, u32[]{:S(2)}) async-start(bf16[8,128,128]{2,1,0:T(8,128)(2,1)} %bitcast.18), calls=%async_computation.1 | async-start | bytes 524288 | tf_op jit(solution)/shard_map/all_to_all | solution.py:74
  328.5 1.3 copy-start.7
  332.0 2.7 copy-start.10
  347.4 6.4 %copy-start.1 = (bf16[1024,1,384]{2,0,1:T(8,128)(2,1)S(1)}, bf16[1024,1,384]{2,0,1:T(8,128)(2,1)}, u32[]{:S(2)}) copy-start(bf16[1024,1,384]{2,0,1:T(8,128)(2,1)} %param.24) | copy-start | bytes 2359300
  (3 other events, 2.6 us)
Sparse Core Ops, SparseCore 0:
  192.2 34.1 all-gather.5
  252.2 34.0 all-gather.7
  312.8 34.5 all-gather.9
